TPU v7x, 768 devices: a whole 4x8x12 slice. The times are simulated.
768 devices in a mesh: row: 8 (over x, core), col: 96 (over y, z).
Axes of the slice: x: 4, y: 8, z: 12, core: 2. Of those that a mesh axis runs over, the one named last changes fastest.
Arguments:
- slab_blocks: bfloat16 [2048, 122880], P('row', 'col'), may hold values from -6 to 6
- slab_pattern: int32 [16, 960], P('row', 'col'), may hold values 0 or 1
- right_blocks: bfloat16 [122880, 3072], P('col', 'row'), may hold values from -0.0546875 to 0.0546875
- right_pattern: int32 [960, 24], P('col', 'row'), may hold values 0 or 1
- atom_sizes: int32 [960], P('col'), may hold values from 64 to 128
Outputs:
- product: float32 [2048, 3072], P('row', 'col')
All inputs are finite; a program needn't handle non-finite values. No bound on the sum of `slab_pattern` or of `right_pattern` on one device may be relied on, other than what follows from the above.
Results may differ from a plain program's by a relative error of at most 0.0003.
Values may be sent and summed in bfloat16 or wider, within the bound.
No kernel may reach another device: no remote copies, remote signals or barrier semaphores. Data moves between devices by JAX's collectives and lax.ppermute only.
A program may use at most 32 MiB of HBM per device.

v0:
```python
import jax
import jax.numpy as jnp
from jax import lax
from jax.sharding import PartitionSpec as P


def orbital_mask(sizes, width):
    inner = jnp.arange(width, dtype=jnp.int32)
    return (inner[None, :] < sizes[:, None]).reshape(-1).astype(jnp.bfloat16)


def shards(slab_blocks, slab_pattern, right_blocks, right_pattern, atom_sizes):
    width = slab_blocks.shape[1] // atom_sizes.shape[0]
    orbitals = orbital_mask(atom_sizes, width)
    left_mask = jnp.repeat(
        jnp.repeat(slab_pattern.astype(jnp.bfloat16), width, axis=0), width, axis=1
    )
    right_mask = jnp.repeat(
        jnp.repeat(right_pattern.astype(jnp.bfloat16), width, axis=0), width, axis=1
    )
    left = slab_blocks * left_mask * orbitals[None, :]
    right = right_blocks * right_mask * orbitals[:, None]
    partial_all = jnp.dot(
        left, lax.all_gather(right, "row", axis=1, tiled=True), preferred_element_type=jnp.float32
    )
    total = lax.psum(partial_all, "col")
    share = total.shape[1] // lax.axis_size("col")
    return lax.dynamic_slice_in_dim(total, lax.axis_index("col") * share, share, 1)


def solution(mesh):
    in_specs = (P("row", "col"), P("row", "col"), P("col", "row"), P("col", "row"), P("col"))
    out_specs = P("row", "col")
    return jax.shard_map(shards, mesh=mesh, in_specs=in_specs, out_specs=out_specs, check_vma=False)
```

profile of v0, /device:TPU:6, one launch (start us, length us, event | category | flops | bytes accessed | tf_op | source)
XLA Modules:
  0.0 335.8 jit_solution(8156988426320948115)
XLA Ops:
  6.5 0.0 all-gather.2.cloned.1.call-start
  6.5 1.5 copy.12
  8.1 0.7 fusion.3
  8.8 0.7 convert_element_type.23
  9.5 0.1 broadcast_bitcast_fusion
  9.6 1.1 fusion
  10.7 0.0 all-gather.2.cloned.1.call-update
  10.8 0.0 all-reduce.2.cloned.1.call-start
  10.8 1.3 copy.11
  12.1 0.7 convert_element_type.20
  12.8 0.1 copy.10
  12.9 0.1 broadcast_bitcast_fusion.1
  13.0 0.2 fusion.1
  13.3 57.9 %all-gather.2.cloned.1.call-done = bf16[1280,3072]{0,1:T(8,128)(2,1)} async-done(((bf16[1280,384]{0,1:T(8,128)(2,1)}), bf16[1280,3072]{0,1:T(8,128)(2,1)}) %all-gather.2.cloned.1.call-update) | async-done | bytes 7864336 | tf_op jit(solution)/shard_map/all_gather | solution.py:24
  71.2 7.2 %fusion.4 = f32[256,3072]{0,1:T(8,128)} fusion(bf16[1280,3072]{0,1:T(8,128)(2,1)} %all-gather.2.cloned.1.call-done, bf16[256,1280]{0,1:T(8,128)(2,1)S(1)} %fusion.1), kind=kOutput, calls=%fused_computation.11 | convolution fusion | flops 2013265920 | bytes 11665408 | tf_op jit(solution)/shard_map/dot_general | solution.py:23
  78.4 0.0 all-reduce.2.cloned.1.call-update
  78.5 249.1 %all-reduce.2.cloned.1.call-done = f32[256,3072]{0,1:T(8,128)} async-done(((f32[256,3072]{0,1:T(8,128)}), f32[256,3072]{0,1:T(8,128)}) %all-reduce.2.cloned.1.call-update) | async-done | bytes 3145744 | tf_op jit(solution)/shard_map/psum | solution.py:26
  327.6 1.4 constant_dynamic-slice_fusion
  (3 shorter events, 0.0 us)
Async XLA Ops:
  6.5 64.7 %all-gather.2.cloned.1.call-start = ((), (), s32[]{:S(2)}) async-start(), calls=%async_computation | async-start | bytes 8847360 | tf_op jit(solution)/shard_map/all_gather | solution.py:24
  10.8 316.8 %all-reduce.2.cloned.1.call-start = ((), (), s32[]{:S(2)}) async-start(), calls=%async_computation.1 | async-start | bytes 6291456 | tf_op jit(solution)/shard_map/psum | solution.py:26
Sparse Core Ops, SparseCore 0:
  10.9 60.3 all-gather.1
  78.6 248.9 all-reduce.1
where the time goes:
time: 336 us
  waiting for transfers between devices  307 us (91%)
  between operations  13.5 us (4%)
  matrix products  7.19 us (2%)
  local copies, waits for them, and re-layouts  4.53 us (1%)
  other arithmetic  3.49 us (1%)
    psum x1, waiting for transfers between devices, shards(): total = lax.psum(partial_all, 'col')  249 us
    all_gather x1, waiting for transfers between devices, shards(): lax.all_gather(right, 'row', axis=1, tiled=True)  57.9 us
    dot_general x1, matrix products, shards(): jnp.dot(left, lax.all_gather(right, 'row', axis=1, tiled=True), preferred...  7.19 us
  transfers between devices with their start and end apart: 2, of which 2 were waited for; matrix products, arithmetic and copies ran while one was open for 1% of the time, Pallas kernels for 0%

commit v1 on v0

v1 whole, which is shorter than its diff:
```python
import jax
import jax.numpy as jnp
from jax import lax
from jax.sharding import Mesh, PartitionSpec as P

ZN = 12


def orbital_mask(sizes, width):
    inner = jnp.arange(width, dtype=jnp.int32)
    return (inner[None, :] < sizes[:, None]).reshape(-1).astype(jnp.bfloat16)


def shards(slab_blocks, slab_pattern, right_blocks, right_pattern, atom_sizes):
    width = slab_blocks.shape[1] // atom_sizes.shape[0]
    orbitals = orbital_mask(atom_sizes, width)
    left_mask = jnp.repeat(jnp.repeat(slab_pattern.astype(jnp.bfloat16), width, axis=0), width, axis=1)
    right_mask = jnp.repeat(jnp.repeat(right_pattern.astype(jnp.bfloat16), width, axis=0), width, axis=1)
    left = slab_blocks * left_mask * orbitals[None, :]
    right = right_blocks * right_mask * orbitals[:, None]
    partial = jnp.dot(left, lax.all_gather(right, "row", axis=1, tiled=True), preferred_element_type=jnp.float32)
    ny, nz = lax.axis_size("y"), lax.axis_size("z")
    rows, cols = partial.shape
    p = partial.reshape(rows, ny, nz, cols // (ny * nz))
    p = lax.psum_scatter(p, FIRST, scatter_dimension=AXES[FIRST], tiled=True)
    p = lax.psum_scatter(p, SECOND, scatter_dimension=AXES[SECOND], tiled=True)
    return p.reshape(rows, -1)


AXES = {"y": 1, "z": 2}
FIRST, SECOND = "y", "z"


def solution(mesh):
    nr, nc = mesh.devices.shape
    view = Mesh(mesh.devices.reshape(nr, nc // ZN, ZN), ("row", "y", "z"))
    col = ("y", "z")
    in_specs = (P("row", col), P("row", col), P(col, "row"), P(col, "row"), P(col))
    out_specs = P("row", col)
    return jax.shard_map(shards, mesh=view, in_specs=in_specs, out_specs=out_specs, check_vma=False)
```

time: 336 us -> 200 us (0.60)
  waiting for transfers between devices: 307 us -> 173 us
    psum x1 -> x0, waiting for transfers between devices: 249 us -> none  [shards(): total = lax.psum(partial_all, 'col')]
    reduce_scatter x0 -> x2, waiting for transfers between devices: none -> 115 us  [the longest x1 60.4 us: shards(): p = lax.psum_scatter(p, SECOND, scatter_dimension=AXES[SECOND], tiled=True)]
  transfers between devices with their start and end apart: 2 -> 3, of which waited for: 2 -> 3; matrix products, arithmetic and copies ran while one was open for 1% -> 1% of each run, Pallas kernels for 0% -> 0%
where the time goes in v1:
time: 200 us
  waiting for transfers between devices  173 us (86%)
  between operations  13.1 us (7%)
  matrix products  7.19 us (4%)
  other arithmetic  3.49 us (2%)
  local copies, waits for them, and re-layouts  3.16 us (2%)
    reduce_scatter x1, waiting for transfers between devices, shards(): p = lax.psum_scatter(p, SECOND, scatter_dimension=AXES[SECOND], tiled=True)  60.4 us
    all_gather x1, waiting for transfers between devices, shards(): lax.all_gather(right, 'row', axis=1, tiled=True)  57.9 us
    reduce_scatter x1, waiting for transfers between devices, shards(): p = lax.psum_scatter(p, FIRST, scatter_dimension=AXES[FIRST], tiled=True)  54.4 us
    dot_general x1, matrix products, shards(): jnp.dot(left, lax.all_gather(right, 'row', axis=1, tiled=True), preferred...  7.19 us
  transfers between devices with their start and end apart: 3, of which 3 were waited for; matrix products, arithmetic and copies ran while one was open for 1% of the time, Pallas kernels for 0%

profile of v1, /device:TPU:6, one launch (start us, length us, event | category | flops | bytes accessed | tf_op | source)
XLA Modules:
  0.0 199.9 jit_solution(15741649599095514538)
XLA Ops:
  6.5 0.0 all-gather.2.cloned.1.call-start
  6.5 0.7 convert_element_type.23
  7.2 0.7 fusion.3
  7.9 0.1 broadcast_bitcast_fusion
  8.0 1.6 copy.14
  9.6 1.1 fusion
  10.7 0.0 all-gather.2.cloned.1.call-update
  10.8 0.0 reduce-scatter.3.cloned.1.call-start
  10.8 0.7 convert_element_type.20
  11.5 0.1 copy.12
  11.6 0.1 broadcast_bitcast_fusion.1
  11.7 1.3 copy.13
  13.0 0.3 fusion.1
  13.3 57.9 %all-gather.2.cloned.1.call-done = bf16[1280,3072]{0,1:T(8,128)(2,1)} async-done(((bf16[1280,384]{0,1:T(8,128)(2,1)}), bf16[1280,3072]{0,1:T(8,128)(2,1)}) %all-gather.2.cloned.1.call-update) | async-done | bytes 7864336 | tf_op jit(solution)/shard_map/all_gather | solution.py:21
  71.2 7.2 %fusion.4 = f32[256,3072]{0,1:T(8,128)} fusion(bf16[1280,3072]{0,1:T(8,128)(2,1)} %all-gather.2.cloned.1.call-done, bf16[256,1280]{0,1:T(8,128)(2,1)S(1)} %fusion.1), kind=kOutput, calls=%fused_computation.10 | convolution fusion | flops 2013265920 | bytes 11665408 | tf_op jit(solution)/shard_map/dot_general | solution.py:21
  78.4 0.0 reduce-scatter.3.cloned.1.call-update
  78.5 0.0 reduce-scatter.5.cloned.1.call-start
  78.5 54.4 %reduce-scatter.3.cloned.1.call-done = f32[256,1,12,32]{0,3,2,1:T(8,128)} async-done(((f32[256,8,12,32]{0,3,2,1:T(8,128)}), f32[256,1,12,32]{0,3,2,1:T(8,128)}) %reduce-scatter.3.cloned.1.call-update) | async-done | bytes 393232 | tf_op jit(solution)/shard_map/reduce_scatter | solution.py:25
  132.9 0.0 reduce-scatter.5.cloned.1.call-update
  133.0 60.4 %reduce-scatter.5.cloned.1.call-done = f32[256,1,1,32]{0,3,2,1:T(8,128)} async-done(((f32[256,1,12,32]{0,3,2,1:T(8,128)}), f32[256,1,1,32]{0,3,2,1:T(8,128)}) %reduce-scatter.5.cloned.1.call-update) | async-done | bytes 32784 | tf_op jit(solution)/shard_map/reduce_scatter | solution.py:26
  (3 shorter events, 0.0 us)
Async XLA Ops:
  6.5 64.7 %all-gather.2.cloned.1.call-start = ((), (), s32[]{:S(2)}) async-start(), calls=%async_computation.2 | async-start | bytes 8847360 | tf_op jit(solution)/shard_map/all_gather | solution.py:21
  10.8 122.2 %reduce-scatter.3.cloned.1.call-start = ((), (), s32[]{:S(2)}) async-start(), calls=%async_computation.3 | async-start | bytes 3538944 | tf_op jit(solution)/shard_map/reduce_scatter | solution.py:25
  78.5 115.0 %reduce-scatter.5.cloned.1.call-start = ((), (), s32[]{:S(2)}) async-start(), calls=%async_computation.4 | async-start | bytes 425984 | tf_op jit(solution)/shard_map/reduce_scatter | solution.py:26
Sparse Core Ops, SparseCore 0:
  10.9 60.3 all-gather.1
  78.6 54.3 reduce-scatter.2
  136.0 57.3 reduce-scatter.4

commit v2 on v1

v2 whole, which is shorter than its diff:
```python
import jax
import jax.numpy as jnp
from jax import lax
from jax.sharding import Mesh, PartitionSpec as P

XN, ZN = 4, 12
GATHER = "flat"
STAGE2 = "a2a"


def orbital_mask(sizes, width):
    inner = jnp.arange(width, dtype=jnp.int32)
    return (inner[None, :] < sizes[:, None]).reshape(-1).astype(jnp.bfloat16)


def gather_right(right):
    if GATHER == "flat":
        return lax.all_gather(right, ("x", "core"), axis=1, tiled=True), False
    g = lax.all_gather(right, "x", axis=1, tiled=True)
    return lax.all_gather(g, "core", axis=1, tiled=True), True


def shards(slab_blocks, slab_pattern, right_blocks, right_pattern, atom_sizes):
    width = slab_blocks.shape[1] // atom_sizes.shape[0]
    orbitals = orbital_mask(atom_sizes, width)
    left_mask = jnp.repeat(jnp.repeat(slab_pattern.astype(jnp.bfloat16), width, axis=0), width, axis=1)
    right_mask = jnp.repeat(jnp.repeat(right_pattern.astype(jnp.bfloat16), width, axis=0), width, axis=1)
    left = slab_blocks * left_mask * orbitals[None, :]
    right = right_blocks * right_mask * orbitals[:, None]
    gathered, swapped = gather_right(right)
    partial = jnp.dot(left, gathered, preferred_element_type=jnp.float32)
    rows, cols = partial.shape
    nx, nk = lax.axis_size("x"), lax.axis_size("core")
    if swapped:
        partial = partial.reshape(rows, nk, nx, cols // (nk * nx)).transpose(0, 2, 1, 3)
    ny, nz = lax.axis_size("y"), lax.axis_size("z")
    p = partial.reshape(rows, ny, nz, cols // (ny * nz))
    p = lax.psum_scatter(p, "y", scatter_dimension=1, tiled=True)
    if STAGE2 == "rs":
        p = lax.psum_scatter(p, "z", scatter_dimension=2, tiled=True)
    elif STAGE2 == "a2a":
        p = lax.all_to_all(p, "z", 2, 2, tiled=True).sum(axis=2, keepdims=True)
    elif STAGE2 == "ar":
        p = lax.dynamic_slice_in_dim(lax.psum(p, "z"), lax.axis_index("z"), 1, axis=2)
    return p.reshape(rows, -1)


def solution(mesh):
    nr, nc = mesh.devices.shape
    view = Mesh(mesh.devices.reshape(XN, nr // XN, nc // ZN, ZN), ("x", "core", "y", "z"))
    row, col = ("x", "core"), ("y", "z")
    in_specs = (P(row, col), P(row, col), P(col, row), P(col, row), P(col))
    out_specs = P(row, col)
    return jax.shard_map(shards, mesh=view, in_specs=in_specs, out_specs=out_specs, check_vma=False)
```

time: 200 us -> 168 us (0.84)
  waiting for transfers between devices: 173 us -> 112 us
  blocking collectives: 0 us -> 26.9 us
    reduce_scatter x2 -> x1, waiting for transfers between devices: 115 us -> 54.4 us  [shards(): p = lax.psum_scatter(p, 'y', scatter_dimension=1, tiled=True)]
    all_to_all x0 -> x1, blocking collectives: none -> 26.9 us  [shards(): p = lax.all_to_all(p, 'z', 2, 2, tiled=True).sum(axis=2, keepdims=True)]
  transfers between devices with their start and end apart: 3 -> 2, of which waited for: 3 -> 2; matrix products, arithmetic and copies ran while one was open for 1% -> 1% of each run, Pallas kernels for 0% -> 0%
where the time goes in v2:
time: 168 us; the launch traced here: 167 us
  waiting for transfers between devices  112 us (67%)
  blocking collectives  26.9 us (16%)
  between operations  13.4 us (8%)
  matrix products  7.18 us (4%)
  other arithmetic  4.14 us (2%)
  local copies, waits for them, and re-layouts  3.16 us (2%)
    all_gather x1, waiting for transfers between devices, gather_right(): return (lax.all_gather(right, ('x', 'core'), axis=1, tiled=True), False)  57.9 us
    reduce_scatter x1, waiting for transfers between devices, shards(): p = lax.psum_scatter(p, 'y', scatter_dimension=1, tiled=True)  54.4 us
    all_to_all x1, blocking collectives, shards(): p = lax.all_to_all(p, 'z', 2, 2, tiled=True).sum(axis=2, keepdims=True)  26.9 us
    dot_general x1, matrix products, shards(): partial = jnp.dot(left, gathered, preferred_element_type=jnp.float32)  7.18 us
  transfers between devices with their start and end apart: 2, of which 2 were waited for; matrix products, arithmetic and copies ran while one was open for 1% of the time, Pallas kernels for 0%

profile of v2, /device:TPU:6, one launch (start us, length us, event | category | flops | bytes accessed | tf_op | source)
XLA Modules:
  0.0 167.2 jit_solution(12114427468018416483)
XLA Ops:
  6.5 0.0 all-gather.2.cloned.1.call-start
  6.5 0.7 convert_element_type.23
  7.2 0.7 fusion.3
  7.9 0.1 broadcast_bitcast_fusion
  8.0 1.6 copy.17
  9.6 1.2 fusion
  10.8 0.0 all-gather.2.cloned.1.call-update
  10.8 0.0 reduce-scatter.2.cloned.1.call-start
  10.8 0.7 convert_element_type.20
  11.5 0.1 copy.15
  11.6 0.1 broadcast_bitcast_fusion.1
  11.7 1.3 copy.16
  13.1 0.3 fusion.1
  13.3 57.9 %all-gather.2.cloned.1.call-done = bf16[1280,3072]{0,1:T(8,128)(2,1)} async-done(((bf16[1280,384]{0,1:T(8,128)(2,1)}), bf16[1280,3072]{0,1:T(8,128)(2,1)}) %all-gather.2.cloned.1.call-update) | async-done | bytes 7864336 | tf_op jit(solution)/shard_map/all_gather | solution.py:18
  71.3 7.2 %fusion.4 = f32[256,3072]{0,1:T(8,128)} fusion(bf16[1280,3072]{0,1:T(8,128)(2,1)} %all-gather.2.cloned.1.call-done, bf16[256,1280]{0,1:T(8,128)(2,1)S(1)} %fusion.1), kind=kOutput, calls=%fused_computation.10 | convolution fusion | flops 2013265920 | bytes 11665408 | tf_op jit(solution)/shard_map/dot_general | solution.py:31
  78.4 0.0 reduce-scatter.2.cloned.1.call-update
  78.5 54.4 %reduce-scatter.2.cloned.1.call-done = f32[256,1,12,32]{0,3,2,1:T(8,128)} async-done(((f32[256,8,12,32]{0,3,2,1:T(8,128)}), f32[256,1,12,32]{0,3,2,1:T(8,128)}) %reduce-scatter.2.cloned.1.call-update) | async-done | bytes 393232 | tf_op jit(solution)/shard_map/reduce_scatter | solution.py:38
  132.9 26.9 %all_to_all.5 = f32[256,1,12,32]{0,3,1,2:T(8,128)S(1)} all-to-all(f32[256,1,12,32]{0,3,1,2:T(8,128)} %bitcast.28), channel_id=1, replica_groups=mesh['x'=4,'core'=2,'y'=8,'z'=12] {'z'}, dimensions={2} | all-to-all | bytes 786432 | tf_op jit(solution)/shard_map/all_to_all | solution.py:42
  159.7 0.6 reduce_sum.9
  (3 shorter events, 0.0 us)
Async XLA Ops:
  6.5 64.7 %all-gather.2.cloned.1.call-start = ((), (), s32[]{:S(2)}) async-start(), calls=%async_computation.2 | async-start | bytes 8847360 | tf_op jit(solution)/shard_map/all_gather | solution.py:18
  10.8 122.1 %reduce-scatter.2.cloned.1.call-start = ((), (), s32[]{:S(2)}) async-start(), calls=%async_computation.3 | async-start | bytes 3538944 | tf_op jit(solution)/shard_map/reduce_scatter | solution.py:38
Sparse Core Ops, SparseCore 0:
  10.9 60.3 all-gather.1
  78.6 54.2 reduce-scatter.1
